TPU v7x, 256 devices: a whole 4x4x8 slice. The times are simulated.
256 devices in a mesh: row: 64 (over x, z_hi, y), col: 4 (over z_lo, core).
Axes of the slice: x: 4, y: 4, z: 8 (z_hi: 4, z_lo: 2; z = z_hi * 2 + z_lo), core: 2. Of those that a mesh axis runs over, the one named last changes fastest.
Arguments:
- img_hidden: bfloat16 [8, 1536, 2432], P(None, 'row', 'col'), may hold values from -6 to 6
- txt_hidden: bfloat16 [8, 128, 2432], P(None, 'row', 'col'), may hold values from -6 to 6
- latent: float32 [8, 1536, 64], P(None, 'row'), may hold values from -6 to 6
- img_mod: float32 [8, 5, 2432], replicated, may hold values from -4 to 4
- txt_mod: float32 [8, 2, 2432], replicated, may hold values from -4 to 4
- qkv_weight: bfloat16 [3, 2432, 2048], P(None, None, 'col'), may hold values from -0.125 to 0.125
- txt_kv_weight: bfloat16 [2, 2432, 2048], P(None, None, 'col'), may hold values from -0.125 to 0.125
- out_weight: bfloat16 [2048, 2432], P('col', 'row'), may hold values from -0.125 to 0.125
- final_weight: bfloat16 [2432, 64], P('col'), may hold values from -0.125 to 0.125
- qk_gains: float32 [3, 64], replicated, may hold values from 1.5 to 9
- txt_len: int32 [8], replicated, may hold values from 1 to 128, as said below
- step_idx: int32 [8], replicated, may hold values from 1 to 28
Outputs:
- advanced: float32 [8, 1536, 64], P(None, 'row')
- denoised: float32 [8, 1536, 64], P(None, 'row')
Inputs may be any that keep to these rules, and one draw needn't show every extreme that they name: `txt_len`: some request has all 128 text tokens live.
All inputs are finite; a program needn't handle non-finite values.
Results may differ from a plain program's by a relative error of at most 0.0044.
The roundings to bfloat16 on the way count: a program that leaves them out, or rounds other values in their place, can miss the bound.
Values may be sent and summed in bfloat16 or wider, within the bound.
No kernel may reach another device: no remote copies, remote signals or barrier semaphores. Data moves between devices by JAX's collectives and lax.ppermute only.
A program may use at most 128 MiB of HBM per device.

v0:
```python
import jax
import jax.numpy as jnp
from jax import lax
from jax.sharding import PartitionSpec as P

D = 2432
HD = 64
STEPS = 28
eps_norm = 1e-06
neg_fill = -1e30


def layer_norm(values):
    average = jnp.mean(values, -1, keepdims=True)
    centred = values - average
    variance = jnp.mean(centred * centred, -1, keepdims=True)
    return centred * lax.rsqrt(variance + eps_norm)


def rms_heads(values, scaling):
    reshaped = values.reshape(values.shape[:-1] + (values.shape[-1] // HD, HD))
    inverse = lax.rsqrt(jnp.mean(reshaped * reshaped, -1, keepdims=True) + eps_norm)
    return (reshaped * inverse * scaling).astype(jnp.bfloat16)


def sigma_at(indices):
    fraction = indices.astype(jnp.float32) / STEPS
    return 3.0 * fraction / (1.0 + 2.0 * fraction)


def attend_all(queries, key_rows, value_rows, allowed):
    scores = jnp.einsum(
        "rqhd,rkhd->rqhk", queries, key_rows, preferred_element_type=jnp.float32
    ) * HD ** (-0.5)
    scores = jnp.where(allowed[:, None, None, :], scores, neg_fill)
    top_score = jnp.max(scores, -1, keepdims=True)
    exp_scores = jnp.where(allowed[:, None, None, :], jnp.exp(scores - top_score), 0.0)
    row_total = jnp.sum(exp_scores, -1)
    weighted = jnp.einsum(
        "rqhk,rkhd->rqhd",
        exp_scores.astype(jnp.bfloat16),
        value_rows,
        preferred_element_type=jnp.float32,
    )
    return (weighted / row_total[..., None]).astype(jnp.bfloat16)


def per_device(
    img_hidden,
    txt_hidden,
    latent,
    img_mod,
    txt_mod,
    qkv_weight,
    txt_kv_weight,
    out_weight,
    final_weight,
    qk_gains,
    txt_len,
    step_idx,
):
    requests = img_hidden.shape[0]
    patches = img_hidden.shape[1]
    text_rows = txt_hidden.shape[1]
    cols_local = qkv_weight.shape[2]
    heads_local = cols_local // HD
    block_len = patches + text_rows
    img_full, txt_full = (
        lax.all_gather(img_hidden, "col", axis=2, tiled=True),
        lax.all_gather(txt_hidden, "col", axis=2, tiled=True),
    )
    img_wide = img_full.astype(jnp.float32)
    normed = (layer_norm(img_wide) * (1.0 + img_mod[:, 1:2, :]) + img_mod[:, 0:1, :]).astype(
        jnp.bfloat16
    )
    flat_rows = normed.reshape(requests * patches, D)
    projected = jnp.einsum("td,cde->cte", flat_rows, qkv_weight, preferred_element_type=jnp.float32)
    queries = rms_heads(projected[0], qk_gains[0]).reshape(requests, patches, heads_local, HD)
    img_keys = rms_heads(projected[1], qk_gains[1]).reshape(requests, patches, heads_local, HD)
    img_values = projected[2].astype(jnp.bfloat16).reshape(requests, patches, heads_local, HD)
    text_normed = (
        layer_norm(txt_full.astype(jnp.float32)) * (1.0 + txt_mod[:, 1:2, :]) + txt_mod[:, 0:1, :]
    ).astype(jnp.bfloat16)
    text_proj = jnp.einsum(
        "rtd,cde->crte", text_normed, txt_kv_weight, preferred_element_type=jnp.float32
    )
    text_keys = rms_heads(text_proj[0], qk_gains[2])
    text_values = text_proj[1].astype(jnp.bfloat16).reshape(requests, text_rows, heads_local, HD)
    key_rows = jnp.concatenate([img_keys, text_keys], 1)
    value_rows = jnp.concatenate([img_values, text_values], 1)
    key_flat = key_rows.reshape(requests, block_len, cols_local)
    value_flat = value_rows.reshape(requests, block_len, cols_local)
    all_keys, all_values = (
        lax.all_gather(key_flat, "row", axis=1, tiled=True),
        lax.all_gather(value_flat, "row", axis=1, tiled=True),
    )
    key_count = all_keys.shape[1]
    positions = jnp.arange(key_count, dtype=jnp.int32)
    gathered_keys = all_keys.reshape(requests, key_count, heads_local, HD)
    gathered_values = all_values.reshape(requests, key_count, heads_local, HD)
    within = positions % block_len
    source = positions // block_len
    text_pos = source * text_rows + within - patches
    attended = attend_all(
        queries,
        gathered_keys,
        gathered_values,
        (within[None, :] < patches) | (text_pos[None, :] < txt_len[:, None]),
    ).reshape(requests * patches, cols_local)
    partial_value = jnp.dot(
        attended,
        lax.all_gather(out_weight, "row", axis=1, tiled=True),
        preferred_element_type=jnp.float32,
    )
    slab_width = img_hidden.shape[2]
    col_index = lax.axis_index("col")
    shared_sum = lax.psum_scatter(partial_value, "col", scatter_dimension=1, tiled=True)
    col_mods = lax.dynamic_slice_in_dim(img_mod, col_index * slab_width, slab_width, 2)
    mixed = img_hidden.astype(jnp.float32) + col_mods[:, 2:3, :] * shared_sum.reshape(
        requests, patches, slab_width
    )
    row_sums, squares = lax.psum((jnp.sum(mixed, -1), jnp.sum(mixed * mixed, -1)), "col")
    row_mean = row_sums / D
    spread = squares / D - row_mean * row_mean
    scaled = (mixed - row_mean[..., None]) * lax.rsqrt(spread[..., None] + eps_norm)
    modulated = (scaled * (1.0 + col_mods[:, 4:5, :]) + col_mods[:, 3:4, :]).astype(jnp.bfloat16)
    velocity = lax.psum(
        jnp.dot(
            modulated.reshape(requests * patches, slab_width),
            final_weight,
            preferred_element_type=jnp.float32,
        ),
        "col",
    )
    velocity = velocity.reshape(requests, patches, latent.shape[2])
    sigma_now = sigma_at(step_idx)[:, None, None]
    sigma_next = sigma_at(step_idx - 1)[:, None, None]
    advanced = latent + (sigma_next - sigma_now) * velocity
    denoised = latent - sigma_now * velocity
    return (advanced, denoised)


def solution(mesh):
    in_specs = (
        P(None, "row", "col"),
        P(None, "row", "col"),
        P(None, "row", None),
        P(),
        P(),
        P(None, None, "col"),
        P(None, None, "col"),
        P("col", "row"),
        P("col", None),
        P(),
        P(),
        P(),
    )
    out_specs = (P(None, "row", None), P(None, "row", None))
    return jax.shard_map(
        per_device, mesh=mesh, in_specs=in_specs, out_specs=out_specs, check_vma=False
    )
```

profile of v0, /device:TPU:1, one launch (start us, length us, event | category | flops | bytes accessed | tf_op | source)
XLA Modules:
  0.0 487.1 jit_solution(12438980188880885017)
XLA Ops:
  7.2 0.0 all-gather.9.cloned.1.call-start
  7.2 0.7 all-gather.9.cloned.1.call-update
  7.9 0.0 all-gather.7.cloned.1.call-start
  8.0 1.0 copy.78
  9.0 12.9 %all_gather.16 = bf16[8,2,2432]{0,1,2:T(2,128)(2,1)S(1)} all-gather(bf16[8,2,608]{0,1,2:T(2,128)(2,1)S(1)} %copy.78), channel_id=1, replica_groups=mesh['row'=64,'col'=4] {'col'}, dimensions={2}, use_global_device_ids=true | all-gather | bytes 97280 | tf_op jit(solution)/shard_map/all_gather | solution.py:70
  21.9 1.1 copy.79
  23.0 0.1 convert_reduce_fusion.1
  23.1 0.2 fusion.39
  23.3 1.1 fusion.73
  24.4 3.2 fusion.24
  27.6 0.1 mul.267
  27.7 0.1 reduce_sum.95
  27.8 0.1 mul.268
  27.9 0.1 mul.269
  28.0 0.1 mul.273
  28.1 0.8 copy.76
  28.9 35.2 %all_gather.15 = bf16[8,24,2432]{1,0,2:T(8,128)(2,1)} all-gather(bf16[8,24,608]{1,0,2:T(8,128)(2,1)S(1)} %copy.76), channel_id=1, replica_groups=mesh['row'=64,'col'=4] {'col'}, dimensions={2}, use_global_device_ids=true | all-gather | bytes 1167360 | tf_op jit(solution)/shard_map/all_gather | solution.py:69
  64.1 4.8 copy.77
  69.0 0.2 convert_reduce_fusion
  69.2 0.4 fusion.17
  69.6 0.9 add_bitcast_fusion
  70.5 0.6 fusion.20
  71.1 4.8 convolution_bitcast_fusion.1
  76.0 0.2 slice_multiply_fusion.1
  76.2 0.8 copy-done.2
  77.0 0.2 copy.84
  77.2 0.1 reduce_sum.94
  77.2 0.1 rsqrt.53
  77.3 0.1 copy.85
  77.4 0.3 mul.258
  77.7 0.2 mul.259
  77.9 0.1 mul.263
  78.0 0.3 fusion.36
  78.3 0.7 pad_maximum_fusion.1
  79.0 0.0 all-gather.5.cloned.1.call-start
  79.1 1.0 slice.80
  80.1 0.1 copy.82
  80.2 0.7 pad_maximum_fusion
  80.9 0.2 reduce-scatter.4.cloned.1.call-start
  81.2 1.1 reshape_squeeze.11
  82.2 0.2 copy.88
  82.4 0.1 reduce_sum.96
  82.5 0.1 rsqrt.56
  82.6 0.1 compare_or_fusion
  82.7 13.0 %all-gather.9.cloned.1.call-done = bf16[64,38,512]{2,1,0:T(8,128)(2,1)} async-done(((bf16[1,38,512]{2,1,0:T(8,128)(2,1)}), bf16[64,38,512]{2,1,0:T(8,128)(2,1)}) %all-gather.9.cloned.1.call-update) | async-done | bytes 2490384 | tf_op jit(solution)/shard_map/all_gather | solution.py:112
  95.8 2.8 reshape.196
  98.5 137.7 %all-gather.7.cloned.1.call-done = bf16[8,1664,512]{2,0,1:T(8,128)(2,1)} async-done(((bf16[8,26,512]{2,0,1:T(8,128)(2,1)}), bf16[8,1664,512]{2,0,1:T(8,128)(2,1)}) %all-gather.7.cloned.1.call-update) | async-done | bytes 13631504 | tf_op jit(solution)/shard_map/all_gather | solution.py:94
  236.3 19.4 %copy.87 = bf16[8,1664,512]{1,2,0:T(8,128)(2,1)} copy(bf16[8,1664,512]{2,0,1:T(8,128)(2,1)} %all-gather.7.cloned.1.call-done) | data formatting | bytes 27262976 | tf_op jit(solution)/shard_map/all_gather | solution.py:94
  255.7 8.9 %fusion.74 = (f32[8,24,8]{1,2,0:T(8,128)S(1)}, bf16[8,24,8,1664]{3,1,2,0:T(8,128)(2,1)}) fusion(pred[8,1664]{1,0:T(8,128)(4,1)S(1)} %compare_or_fusion, bf16[8,1664,8,64]{1,3,2,0:T(8,128)(2,1)} %bitcast.107, f32[8,24,8,64]{3,2,1,0:T(8,128)} %reshape_squeeze.11, f32[64]{0:T(128)S(1)} %get-tuple-element.23, f32[8,24,8]{1,2,0:T(8,128)S(1)} %copy.89), kind=kOutput, calls=%fused_computation.107 | convolution fusion | flops 342787712 | bytes 19162368 | tf_op jit(solution)/shard_map/sub | solution.py:37
  264.6 122.3 %all-gather.5.cloned.1.call-done = bf16[8,1664,512]{2,0,1:T(8,128)(2,1)} async-done(((bf16[8,26,512]{2,0,1:T(8,128)(2,1)}), bf16[8,1664,512]{2,0,1:T(8,128)(2,1)}) %all-gather.5.cloned.1.call-update) | async-done | bytes 13631504 | tf_op jit(solution)/shard_map/all_gather | solution.py:95
  386.9 19.4 %copy.83 = bf16[8,1664,512]{1,2,0:T(8,128)(2,1)} copy(bf16[8,1664,512]{2,0,1:T(8,128)(2,1)} %all-gather.5.cloned.1.call-done) | data formatting | bytes 27262976 | tf_op jit(solution)/shard_map/all_gather | solution.py:95
  406.3 8.4 %fusion.30 = bf16[8,24,8,64]{3,1,2,0:T(8,128)(2,1)S(1)} fusion(bf16[8,1664,8,64]{1,3,2,0:T(8,128)(2,1)} %bitcast.108, bf16[8,24,8,1664]{3,1,2,0:T(8,128)(2,1)} %get-tuple-element.27, f32[8,24,8]{1,2,0:T(8,128)S(1)} %get-tuple-element.26), kind=kOutput, calls=%fused_computation.28 | convolution fusion | flops 327352320 | bytes 18946048 | tf_op jit(solution)/shard_map/rqhk,rkhd->rqhd/dot_general | solution.py:39
  414.7 0.1 copy.91
  414.8 0.3 reshape.191
  415.1 2.3 convolution_bitcast_fusion
  417.4 0.9 dynamic-slice_bitcast_fusion.1
  418.2 42.7 %reduce-scatter.4.cloned.1.call-done = f32[608,192]{1,0:T(8,128)} async-done(((f32[2432,192]{1,0:T(8,128)}), f32[608,192]{1,0:T(8,128)}) %reduce-scatter.4.cloned.1.call-update) | async-done | bytes 466960
  461.0 1.3 copy.96
  462.3 0.2 fusion.43
  462.4 5.5 %all-reduce = (f32[8,24]{1,0:T(8,128)S(1)}, f32[8,24]{1,0:T(8,128)S(1)}) all-reduce(f32[8,24]{1,0:T(8,128)S(1)} %get-tuple-element.3, f32[8,24]{1,0:T(8,128)S(1)} %get-tuple-element.2), channel_id=1, replica_groups=mesh['row'=64,'col'=4] {'col'}, use_global_device_ids=true, to_apply=%region_13.14 | all-reduce | flops 384 | bytes 3072 | tf_op jit(solution)/shard_map/psum | solution.py:122
  467.9 0.2 add_convert_fusion
  468.2 0.2 fusion.79
  468.4 11.5 %psum.23 = f32[8,24,64]{2,1,0:T(8,128)S(1)} all-reduce(f32[8,24,64]{2,1,0:T(8,128)S(1)} %bitcast.118), channel_id=1, replica_groups=mesh['row'=64,'col'=4] {'col'}, use_global_device_ids=true, to_apply=%region_14.15 | all-reduce | flops 12288 | bytes 98304 | tf_op jit(solution)/shard_map/psum | solution.py:127
  479.9 0.8 multiply_subtract_fusion
  (35 shorter events, 0.2 us)
Async XLA Ops:
  7.2 461.0 %copy-start = (bf16[608,64]{0,1:T(8,128)(2,1)S(1)}, bf16[608,64]{0,1:T(8,128)(2,1)}, u32[]{:S(2)}) copy-start(bf16[608,64]{0,1:T(8,128)(2,1)} %param.20) | copy-start | bytes 233476
  7.2 20.8 %copy-start.4 = (f32[3,64]{1,0:T(4,128)S(1)}, f32[3,64]{1,0:T(4,128)}, u32[]{:S(2)}) copy-start(f32[3,64]{1,0:T(4,128)} %param.21) | copy-start | bytes 2308
  7.2 20.9 %copy-start.1 = (bf16[8,24,608]{2,1,0:T(8,128)(2,1)S(1)}, bf16[8,24,608]{2,1,0:T(8,128)(2,1)}, u32[]{:S(2)}) copy-start(bf16[8,24,608]{2,1,0:T(8,128)(2,1)} %param.12) | copy-start | bytes 700420
  7.2 88.6 %all-gather.9.cloned.1.call-start = ((), (), s32[]{:S(2)}) async-start(), calls=%async_computation.3 | async-start | bytes 2662400 | tf_op jit(solution)/shard_map/all_gather | solution.py:112
  7.9 228.3 %all-gather.7.cloned.1.call-start = ((), (), s32[]{:S(2)}) async-start(), calls=%async_computation.2 | async-start | bytes 13844480 | tf_op jit(solution)/shard_map/all_gather | solution.py:94
  76.0 1.0 copy-start.2
  77.0 5.7 %copy-start.5 = (s32[8]{0:T(128)S(1)}, s32[8]{0:T(128)}, u32[]{:S(2)}) copy-start(s32[8]{0:T(128)} %param.22) | copy-start | bytes 100
  79.0 307.9 %all-gather.5.cloned.1.call-start = ((), (), s32[]{:S(2)}) async-start(), calls=%async_computation.1 | async-start | bytes 13844480 | tf_op jit(solution)/shard_map/all_gather | solution.py:95
  80.9 380.0 %reduce-scatter.4.cloned.1.call-start = ((), (), s32[]{:S(2)}) async-start(), calls=%async_computation.4 | async-start | bytes 3112960
  414.8 3.5 copy-start.6
  415.0 64.8 %copy-start.3 = (f32[8,24,64]{2,1,0:T(8,128)S(1)}, f32[8,24,64]{2,1,0:T(8,128)}, u32[]{:S(2)}) copy-start(f32[8,24,64]{2,1,0:T(8,128)} %param.14) | copy-start | bytes 147460
Sparse Core Ops, SparseCore 0:
  11.3 84.3 all-gather.8
  99.0 137.1 all-gather.6
  239.6 147.2 all-gather.4
  417.5 43.4 reduce-scatter.3
where the time goes:
time: 489 us; the launch traced here: 487 us
  waiting for transfers between devices  317 us (65%)
  blocking collectives  65 us (13%)
  local copies, waits for them, and re-layouts  56.6 us (12%)
  matrix products  27.8 us (6%)
  between operations  14.2 us (3%)
  other arithmetic  6.71 us (1%)
    all_gather x1, waiting for transfers between devices, per_device(): lax.all_gather(key_flat, 'row', axis=1, tiled=True)  138 us
    all_gather x1, waiting for transfers between devices, per_device(): lax.all_gather(value_flat, 'row', axis=1, tiled=True)  122 us
    unnamed x5, waiting for transfers between devices  43.4 us
    all_gather x1, blocking collectives, per_device(): lax.all_gather(img_hidden, 'col', axis=2, tiled=True)  35.2 us
    all_gather x1, local copies, waits for them, and re-layouts, per_device(): lax.all_gather(key_flat, 'row', axis=1, tiled=True)  19.4 us
    all_gather x1, local copies, waits for them, and re-layouts, per_device(): lax.all_gather(value_flat, 'row', axis=1, tiled=True)  19.4 us
    all_gather x1, waiting for transfers between devices, per_device(): lax.all_gather(out_weight, 'row', axis=1, tiled=True)  13 us
    all_gather x1, blocking collectives, per_device(): lax.all_gather(txt_hidden, 'col', axis=2, tiled=True)  12.9 us
  transfers between devices with their start and end apart: 4, of which 4 were waited for; matrix products, arithmetic and copies ran while one was open for 12% of the time, Pallas kernels for 0%

commit v1 on v0

--- a/solution.py
+++ b/solution.py
@@ -66,7 +66,9 @@
     heads_local = cols_local // HD
     block_len = patches + text_rows
     img_full, txt_full = (
-        lax.all_gather(img_hidden, "col", axis=2, tiled=True),
+        jnp.concatenate(
+            lax.all_to_all(jnp.stack([img_hidden] * lax.axis_size("col")), "col", 0, 0), axis=2
+        ),
         lax.all_gather(txt_hidden, "col", axis=2, tiled=True),
     )
     img_wide = img_full.astype(jnp.float32)

time: 489 us -> 494 us (1.010)
  blocking collectives: 65 us -> 36.4 us
  waiting for transfers between devices: 317 us -> 344 us
  starting transfers between devices: 0.34 us -> 7.02 us
    all_gather x1 -> x0, blocking collectives: 35.2 us -> none  [per_device(): lax.all_gather(img_hidden, 'col', axis=2, tiled=True)]
    all_gather x1, waiting for transfers between devices: 13 us -> 40.6 us  [per_device(): lax.all_gather(out_weight, 'row', axis=1, tiled=True)]
    all_to_all x0 -> x1, starting transfers between devices: none -> 6.72 us  [per_device(): lax.all_to_all(jnp.stack([img_hidden] * lax.axis_size('col')), 'col', 0, 0)]
    all_gather x1, blocking collectives: 12.9 us -> 19.4 us  [per_device(): lax.all_gather(txt_hidden, 'col', axis=2, tiled=True)]
  transfers between devices with their start and end apart: 4 -> 5, of which waited for: 4 -> 4; matrix products, arithmetic and copies ran while one was open for 12% -> 11% of each run, Pallas kernels for 0% -> 0%
where the time goes in v1:
time: 494 us; the launch traced here: 493 us
  waiting for transfers between devices  344 us (70%)
  local copies, waits for them, and re-layouts  54.8 us (11%)
  blocking collectives  36.4 us (7%)
  matrix products  27.7 us (6%)
  between operations  14.2 us (3%)
  other arithmetic  8.26 us (2%)
  starting transfers between devices  7.02 us (1%)
    all_gather x1, waiting for transfers between devices, per_device(): lax.all_gather(key_flat, 'row', axis=1, tiled=True)  138 us
    all_gather x1, waiting for transfers between devices, per_device(): lax.all_gather(value_flat, 'row', axis=1, tiled=True)  122 us
    unnamed x5, waiting for transfers between devices  43.5 us
    all_gather x1, waiting for transfers between devices, per_device(): lax.all_gather(out_weight, 'row', axis=1, tiled=True)  40.6 us
    all_gather x1, blocking collectives, per_device(): lax.all_gather(txt_hidden, 'col', axis=2, tiled=True)  19.4 us
    all_gather x1, local copies, waits for them, and re-layouts, per_device(): lax.all_gather(value_flat, 'row', axis=1, tiled=True)  19.4 us
    all_gather x1, local copies, waits for them, and re-layouts, per_device(): lax.all_gather(key_flat, 'row', axis=1, tiled=True)  19.4 us
    psum x1, blocking collectives, per_device(): lax.psum(jnp.dot(modulated.reshape(requests * patches, slab_width), final...  11.5 us
  transfers between devices with their start and end apart: 5, of which 4 were waited for; matrix products, arithmetic and copies ran while one was open for 11% of the time, Pallas kernels for 0%

profile of v1, /device:TPU:1, one launch (start us, length us, event | category | flops | bytes accessed | tf_op | source)
XLA Modules:
  0.0 492.6 jit_solution(13732701123297076356)
XLA Ops:
  7.2 2.1 stack.2
  9.2 6.7 %all-to-all-start = ((bf16[4,8,24,608]{3,2,1,0:T(8,128)(2,1)}), bf16[4,8,24,608]{3,2,1,0:T(8,128)(2,1)S(1)}, u32[]{:S(2)}, u32[]{:S(2)}) async-start(bf16[4,8,24,608]{3,2,1,0:T(8,128)(2,1)} %stack.2), calls=%async_computation | async-start | bytes 1966080 | tf_op jit(solution)/shard_map/all_to_all | solution.py:70
  16.0 0.7 all-gather.9.cloned.1.call-update
  16.7 1.0 copy.72
  17.8 19.4 %all_gather.12 = bf16[8,2,2432]{0,1,2:T(2,128)(2,1)S(1)} all-gather(bf16[8,2,608]{0,1,2:T(2,128)(2,1)S(1)} %copy.72), channel_id=1, replica_groups=mesh['row'=64,'col'=4] {'col'}, dimensions={2}, use_global_device_ids=true | all-gather | bytes 97280 | tf_op jit(solution)/shard_map/all_gather | solution.py:72
  37.2 1.1 copy.73
  38.3 0.1 convert_reduce_fusion
  38.4 0.1 fusion.70
  38.5 0.2 fusion.36
  38.7 3.2 fusion.19
  42.0 0.1 mul.273
  42.0 0.1 reduce_sum.95
  42.2 0.1 mul.274
  42.2 0.1 mul.275
  42.3 0.1 mul.279
  42.4 0.1 mul.269
  42.5 0.9 add_bitcast_fusion
  43.5 0.2 fusion.22
  43.7 0.1 div.61
  43.8 0.4 multiply_reduce_fusion
  44.2 0.1 rsqrt.54
  44.3 0.1 convert_bitcast_fusion
  44.4 1.3 copy.71
  45.7 2.3 reshape.214
  48.0 2.0 fusion.15
  50.0 4.8 convolution_bitcast_fusion.1
  54.8 0.2 slice_multiply_fusion.1
  55.0 0.8 copy-done.2
  55.8 0.2 copy.78
  56.0 0.1 reduce_sum.94
  56.1 0.1 rsqrt.57
  56.2 0.1 copy.79
  56.3 0.3 mul.264
  56.5 0.2 mul.265
  56.8 0.3 fusion.33
  57.0 0.7 pad_maximum_fusion.1
  57.8 1.0 slice.80
  58.9 0.1 copy.76
  58.9 0.7 pad_maximum_fusion
  59.7 0.2 reduce-scatter.4.cloned.1.call-start
  60.0 0.1 compare_or_fusion
  60.1 0.2 reshape_squeeze.11
  60.2 0.2 copy.82
  60.5 0.1 rsqrt.60
  60.6 40.6 %all-gather.9.cloned.1.call-done = bf16[64,38,512]{2,1,0:T(8,128)(2,1)} async-done(((bf16[1,38,512]{2,1,0:T(8,128)(2,1)}), bf16[64,38,512]{2,1,0:T(8,128)(2,1)}) %all-gather.9.cloned.1.call-update) | async-done | bytes 2490384 | tf_op jit(solution)/shard_map/all_gather | solution.py:114
  101.2 2.8 reshape.216
  104.0 137.7 %all-gather.7.cloned.1.call-done = bf16[8,1664,512]{2,0,1:T(8,128)(2,1)} async-done(((bf16[8,26,512]{2,0,1:T(8,128)(2,1)}), bf16[8,1664,512]{2,0,1:T(8,128)(2,1)}) %all-gather.7.cloned.1.call-update) | async-done | bytes 13631504 | tf_op jit(solution)/shard_map/all_gather | solution.py:96
  241.8 19.4 %copy.81 = bf16[8,1664,512]{1,2,0:T(8,128)(2,1)} copy(bf16[8,1664,512]{2,0,1:T(8,128)(2,1)} %all-gather.7.cloned.1.call-done) | data formatting | bytes 27262976 | tf_op jit(solution)/shard_map/all_gather | solution.py:96
  261.1 8.8 %fusion.71 = (f32[8,24,8]{1,2,0:T(8,128)S(1)}, bf16[8,24,8,1664]{3,1,2,0:T(8,128)(2,1)}) fusion(pred[8,1664]{1,0:T(8,128)(4,1)S(1)} %compare_or_fusion, bf16[8,1664,8,64]{1,3,2,0:T(8,128)(2,1)} %bitcast.120, f32[8,24,8,64]{3,2,1,0:T(8,128)S(1)} %reshape_squeeze.11, f32[64]{0:T(128)S(1)} %get-tuple-element.23, f32[8,24,8]{1,2,0:T(8,128)S(1)} %copy.83), kind=kOutput, calls=%fused_computation.106 | convolution fusion | flops 342787712 | bytes 19162368 | tf_op jit(solution)/shard_map/sub | solution.py:37
  270.0 122.4 %all-gather.5.cloned.1.call-done = bf16[8,1664,512]{2,0,1:T(8,128)(2,1)} async-done(((bf16[8,26,512]{2,0,1:T(8,128)(2,1)}), bf16[8,1664,512]{2,0,1:T(8,128)(2,1)}) %all-gather.5.cloned.1.call-update) | async-done | bytes 13631504 | tf_op jit(solution)/shard_map/all_gather | solution.py:97
  392.4 19.4 %copy.77 = bf16[8,1664,512]{1,2,0:T(8,128)(2,1)} copy(bf16[8,1664,512]{2,0,1:T(8,128)(2,1)} %all-gather.5.cloned.1.call-done) | data formatting | bytes 27262976 | tf_op jit(solution)/shard_map/all_gather | solution.py:97
  411.8 8.4 %fusion.26 = bf16[8,24,8,64]{3,1,2,0:T(8,128)(2,1)S(1)} fusion(bf16[8,1664,8,64]{1,3,2,0:T(8,128)(2,1)} %bitcast.121, bf16[8,24,8,1664]{3,1,2,0:T(8,128)(2,1)} %get-tuple-element.27, f32[8,24,8]{1,2,0:T(8,128)S(1)} %get-tuple-element.26), kind=kOutput, calls=%fused_computation.26 | convolution fusion | flops 327352320 | bytes 18946048 | tf_op jit(solution)/shard_map/rqhk,rkhd->rqhd/dot_general | solution.py:39
  420.2 0.1 copy.85
  420.3 0.3 reshape.210
  420.6 2.3 convolution_bitcast_fusion
  422.9 0.9 dynamic-slice_bitcast_fusion.1
  423.8 42.7 %reduce-scatter.4.cloned.1.call-done = f32[608,192]{1,0:T(8,128)} async-done(((f32[2432,192]{1,0:T(8,128)}), f32[608,192]{1,0:T(8,128)}) %reduce-scatter.4.cloned.1.call-update) | async-done | bytes 466960
  466.4 1.3 copy.90
  467.8 0.2 fusion.40
  467.9 5.5 %all-reduce = (f32[8,24]{1,0:T(8,128)S(1)}, f32[8,24]{1,0:T(8,128)S(1)}) all-reduce(f32[8,24]{1,0:T(8,128)S(1)} %get-tuple-element.3, f32[8,24]{1,0:T(8,128)S(1)} %get-tuple-element.2), channel_id=1, replica_groups=mesh['row'=64,'col'=4] {'col'}, use_global_device_ids=true, to_apply=%region_13.14 | all-reduce | flops 384 | bytes 3072 | tf_op jit(solution)/shard_map/psum | solution.py:124
  473.4 0.2 add_convert_fusion
  473.6 0.2 fusion.76
  473.9 11.5 %psum.23 = f32[8,24,64]{2,1,0:T(8,128)S(1)} all-reduce(f32[8,24,64]{2,1,0:T(8,128)S(1)} %bitcast.130), channel_id=1, replica_groups=mesh['row'=64,'col'=4] {'col'}, use_global_device_ids=true, to_apply=%region_14.15 | all-reduce | flops 12288 | bytes 98304 | tf_op jit(solution)/shard_map/psum | solution.py:129
  485.3 0.8 multiply_subtract_fusion
  (42 shorter events, 0.4 us)
Async XLA Ops:
  7.2 466.5 %copy-start = (bf16[608,64]{0,1:T(8,128)(2,1)S(1)}, bf16[608,64]{0,1:T(8,128)(2,1)}, u32[]{:S(2)}) copy-start(bf16[608,64]{0,1:T(8,128)(2,1)} %param.20) | copy-start | bytes 233476
  7.2 31.2 %copy-start.3 = (f32[8,2,2432]{2,1,0:T(2,128)S(1)}, f32[8,2,2432]{2,1,0:T(2,128)}, u32[]{:S(2)}) copy-start(f32[8,2,2432]{2,1,0:T(2,128)} %param.16) | copy-start | bytes 466948
  9.2 34.2 %all-to-all-start = ((bf16[4,8,24,608]{3,2,1,0:T(8,128)(2,1)}), bf16[4,8,24,608]{3,2,1,0:T(8,128)(2,1)S(1)}, u32[]{:S(2)}, u32[]{:S(2)}) async-start(bf16[4,8,24,608]{3,2,1,0:T(8,128)(2,1)} %stack.2), calls=%async_computation | async-start | bytes 1966080 | tf_op jit(solution)/shard_map/all_to_all | solution.py:70
  16.0 26.4 %copy-start.5 = (f32[3,64]{1,0:T(4,128)S(1)}, f32[3,64]{1,0:T(4,128)}, u32[]{:S(2)}) copy-start(f32[3,64]{1,0:T(4,128)} %param.21) | copy-start | bytes 2308
  16.0 85.3 %all-gather.9.cloned.1.call-start = ((), (), s32[]{:S(2)}) async-start(), calls=%async_computation.4 | async-start | bytes 2662400 | tf_op jit(solution)/shard_map/all_gather | solution.py:114
  16.7 225.1 %all-gather.7.cloned.1.call-start = ((), (), s32[]{:S(2)}) async-start(), calls=%async_computation.3 | async-start | bytes 13844480 | tf_op jit(solution)/shard_map/all_gather | solution.py:96
  54.8 1.0 copy-start.2
  54.8 5.2 %copy-start.6 = (s32[8]{0:T(128)S(1)}, s32[8]{0:T(128)}, u32[]{:S(2)}) copy-start(s32[8]{0:T(128)} %param.22) | copy-start | bytes 100
  57.8 334.6 %all-gather.5.cloned.1.call-start = ((), (), s32[]{:S(2)}) async-start(), calls=%async_computation.2 | async-start | bytes 13844480 | tf_op jit(solution)/shard_map/all_gather | solution.py:97
  59.7 406.8 %reduce-scatter.4.cloned.1.call-start = ((), (), s32[]{:S(2)}) async-start(), calls=%async_computation.5 | async-start | bytes 3112960
  420.3 3.5 copy-start.7
  420.5 47.2 %copy-start.1 = (bf16[8,24,608]{2,1,0:T(8,128)(2,1)S(1)}, bf16[8,24,608]{2,1,0:T(8,128)(2,1)}, u32[]{:S(2)}) copy-start(bf16[8,24,608]{2,1,0:T(8,128)(2,1)} %param.12) | copy-start | bytes 700420
  420.5 64.8 %copy-start.4 = (f32[8,24,64]{2,1,0:T(8,128)S(1)}, f32[8,24,64]{2,1,0:T(8,128)}, u32[]{:S(2)}) copy-start(f32[8,24,64]{2,1,0:T(8,128)} %param.14) | copy-start | bytes 147460
Sparse Core Ops, SparseCore 0:
  20.1 81.0 all-gather.8
  104.5 137.1 all-gather.6
  245.1 147.3 all-gather.4
  423.0 43.4 reduce-scatter.3
